TPU v7x, 128 devices: a whole 4x4x4 slice. The times are simulated.
128 devices in a mesh: chan: 32 (over x, y_lo, z), blk: 4 (over y_hi, core).
Axes of the slice: x: 4, y: 4 (y_hi: 2, y_lo: 2; y = y_hi * 2 + y_lo), z: 4, core: 2. Of those that a mesh axis runs over, the one named last changes fastest.
Arguments:
- voltages: int32 [2048, 134656], P(('chan', 'blk')), may hold values from -128 to 127
- flags: int32 [2048], P(('chan', 'blk')), may hold values 0 or 1
- model_amp: float32 [128, 2048], P('chan'), may hold values from 0.04 to 0.4
- model_phase: float32 [128, 2048], P('chan'), may hold values from -3.140625 to 3.140625
Outputs:
- visibility: bfloat16 [2, 128, 2048, 2048], P(None, 'chan', 'blk')
- gains: float32 [2, 128, 2048], P(None, None, ('chan', 'blk'))
All inputs are finite; a program needn't handle non-finite values. No bound on the sum of `flags` on one device may be relied on, other than what follows from the above.
Results may differ from a plain program's by a relative error of at most 0.0091.
Values may be sent and summed in bfloat16 or wider, within the bound.
No kernel may reach another device: no remote copies, remote signals or barrier semaphores. Data moves between devices by JAX's collectives and lax.ppermute only.
A program may use at most 256 MiB of HBM per device.

v0:
```python
import math
import jax
import jax.numpy as jnp
from jax import lax
from jax.sharding import PartitionSpec as P

CHANS = 128
FRAME = 512
TAPS = 8
BAND_START = 64
SPECTRA = 256
ITERS = 10


def window_table():
    index = jnp.arange(TAPS * FRAME, dtype=jnp.float32)
    offset = (index - TAPS * FRAME / 2 + 0.5) / FRAME
    taper = 0.5 - 0.5 * jnp.cos(2.0 * math.pi * (index + 0.5) / (TAPS * FRAME))
    return (jnp.sinc(offset) * taper).reshape(TAPS, FRAME)


def transform_table():
    sample = jnp.arange(FRAME, dtype=jnp.int32)
    channel = BAND_START + jnp.arange(CHANS, dtype=jnp.int32)
    angle = (sample[:, None] * channel[None, :] % FRAME).astype(jnp.float32) * (
        2.0 * math.pi / FRAME
    )
    return jnp.stack([jnp.cos(angle), -jnp.sin(angle)], axis=1).astype(jnp.bfloat16)


def channelize(voltages, keep):
    window = window_table()
    table = transform_table()
    count = voltages.shape[0]
    samples = voltages.astype(jnp.float32).reshape(count, SPECTRA + TAPS - 1, FRAME)
    frames = window[0] * samples[:, 0:SPECTRA, :]
    for tap in range(1, TAPS):
        frames = frames + window[tap] * samples[:, tap : tap + SPECTRA, :]
    frames = frames.astype(jnp.bfloat16)
    spectra = jnp.einsum("itj,jrc->cirt", frames, table, preferred_element_type=jnp.float32)
    scale = 1.0 / (64.0 * math.sqrt(FRAME))
    return (spectra * (scale * keep)[None, :, None, None]).astype(jnp.bfloat16)


def update_gains(model_re, model_im, power, product_re, product_im):
    denominator = (model_re * model_re + model_im * model_im) * (power[:, None] + 1e-06)
    new_re = (model_re * product_re + model_im * product_im) / denominator
    new_im = (model_re * product_im - model_im * product_re) / denominator
    return (new_re, new_im)


def shards(voltages, flags, model_amp, model_phase):
    keep = (1 - flags).astype(jnp.float32)
    input_count = voltages.shape[0]
    spectra = channelize(voltages, keep)
    blk_count = lax.axis_size("blk")
    block_index = lax.axis_index("blk")
    grouped = lax.all_gather(spectra, "blk", axis=1, tiled=True)
    turned = lax.all_to_all(grouped, "chan", split_axis=0, concat_axis=1, tiled=True)
    local_chans = turned.shape[0]
    all_inputs = turned.shape[1]
    row_count = all_inputs // blk_count
    whole = turned.reshape(local_chans, all_inputs, 2 * SPECTRA)
    rows = lax.dynamic_slice_in_dim(whole, block_index * row_count, row_count, 1)
    rotated = jnp.concatenate([rows[:, :, SPECTRA:], -rows[:, :, :SPECTRA]], axis=2)
    stacked = jnp.stack([rows, rotated])
    correlation = (
        jnp.einsum("rcpk,cqk->rcpq", stacked, whole, preferred_element_type=jnp.float32) / SPECTRA
    )
    visibility = correlation.astype(jnp.bfloat16)
    high = lax.Precision.HIGHEST
    full_re = model_amp * jnp.cos(model_phase)
    full_im = model_amp * jnp.sin(model_phase)
    model_re = lax.dynamic_slice_in_dim(full_re, block_index * row_count, row_count, 1)
    model_im = lax.dynamic_slice_in_dim(full_im, block_index * row_count, row_count, 1)

    def sweep(gain_re, gain_im):
        probe_re = gain_re * model_re - gain_im * model_im
        probe_im = gain_re * model_im + gain_im * model_re
        probes = lax.all_gather(jnp.stack([probe_re, probe_im]), "blk", axis=2, tiled=True)
        power = jnp.sum(probes * probes, axis=(0, 2))
        products = jnp.einsum("rcpq,scq->rscp", correlation, probes, precision=high)
        product_re = products[0, 0] - products[1, 1]
        product_im = products[0, 1] + products[1, 0]
        return update_gains(model_re, model_im, power, product_re, product_im)

    def paired(step_index, carried):
        first_re, first_im = sweep(carried[0], carried[1])
        second_re, second_im = sweep(first_re, first_im)
        return (0.5 * (second_re + first_re), 0.5 * (second_im + first_im))

    start_re = jnp.ones((local_chans, row_count), jnp.float32)
    start_im = jnp.zeros((local_chans, row_count), jnp.float32)
    gain_re, gain_im = lax.fori_loop(0, ITERS // 2, paired, (start_re, start_im))
    solved = lax.all_gather(jnp.stack([gain_re, gain_im]), "blk", axis=2, tiled=True)
    owners = lax.all_to_all(solved, "chan", split_axis=2, concat_axis=1, tiled=True)
    gains = lax.dynamic_slice_in_dim(owners, block_index * input_count, input_count, 2)
    return (visibility, gains)


def solution(mesh):
    return jax.shard_map(
        shards,
        mesh=mesh,
        in_specs=(P(("chan", "blk"), None), P(("chan", "blk")), P("chan", None), P("chan", None)),
        out_specs=(P(None, "chan", "blk", None), P(None, None, ("chan", "blk"))),
        check_vma=False,
    )
```

profile of v0, /device:TPU:1, one launch (start us, length us, event | category | flops | bytes accessed | tf_op | source)
XLA Modules:
  0.0 805.5 jit_solution(235510974840824915)
XLA Ops:
  7.3 1.2 cosine_convert_fusion
  8.6 5.9 convert_element_type.41
  14.5 10.1 %reshape.358 = f32[16,263,512]{2,1,0:T(8,128)} reshape(f32[16,134656]{1,0:T(8,128)} %convert_element_type.41) | data formatting | bytes 17235968 | tf_op jit(solution)/shard_map/reshape | solution.py:35
  24.6 27.3 %fusion.34 = bf16[128,16,2,256]{3,0,1,2:T(8,128)(2,1)} fusion(f32[16]{0:T(128)S(1)} %convert_multiply_fusion, f32[16,263,512]{2,1,0:T(8,128)} %reshape.358, f32[512]{0:T(512)S(1)} %get-tuple-element.223, f32[512]{0:T(512)S(1)} %get-tuple-element.224, f32[512]{0:T(512)S(1)} %get-tuple-element.225, f32[512]{0:T(512)S(1)} %get-tuple-element.226, ...), kind=kOutput, calls=%fused_computation.70 | convolution fusion | flops 1109917696 | bytes 69484608 | tf_op jit(solution)/shard_map/itj,jrc->cirt/dot_general | solution.py:40
  52.0 66.1 %all-gather.2.cloned.1.call-done = bf16[128,64,2,256]{3,0,1,2:T(8,128)(2,1)} async-done(((bf16[128,16,2,256]{3,0,1,2:T(8,128)(2,1)}), bf16[128,64,2,256]{3,0,1,2:T(8,128)(2,1)}) %all-gather.2.cloned.1.call-update) | async-done | bytes 8388624 | tf_op jit(solution)/shard_map/all_gather | solution.py:58
  118.1 11.5 %copy.43 = bf16[128,64,2,256]{3,1,2,0:T(8,128)(2,1)} copy(bf16[128,64,2,256]{3,0,1,2:T(8,128)(2,1)} %all-gather.2.cloned.1.call-done) | data formatting | bytes 16777216 | tf_op jit(solution)/shard_map/all_gather | solution.py:58
  129.7 7.3 all-to-all-start
  137.0 0.8 multiply_add_fusion.2
  137.8 117.2 %all-to-all-done = bf16[128,64,2,256]{3,1,2,0:T(8,128)(2,1)} async-done(((bf16[128,64,2,256]{3,1,2,0:T(8,128)(2,1)}), bf16[128,64,2,256]{3,1,2,0:T(8,128)(2,1)}, u32[]{:S(2)}, u32[]{:S(2)}) %all-to-all-start) | async-done | bytes 8388640 | tf_op jit(solution)/shard_map/all_to_all | solution.py:59
  254.9 16.4 %copy.81 = bf16[32,4,64,2,256]{4,3,2,0,1:T(2,128)(2,1)} copy(bf16[32,4,64,2,256]{4,2,3,1,0:T(8,128)(2,1)} %bitcast.4) | data formatting | bytes 16777216 | tf_op jit(solution)/shard_map/all_to_all | solution.py:59
  271.4 14.1 %reshape.359 = bf16[4,2048,512]{2,1,0:T(8,128)(2,1)} reshape(bf16[4,32,64,2,256]{4,3,2,1,0:T(2,128)(2,1)} %bitcast.199) | data formatting | bytes 16777216 | tf_op jit(solution)/shard_map/reshape | solution.py:63
  285.4 14.1 %reshape.366 = bf16[4,2048,512,1]{2,1,0,3:T(8,128)(2,1)} reshape(bf16[4,32,64,2,256]{4,3,2,1,0:T(2,128)(2,1)} %bitcast.200) | data formatting | bytes 16777216 | tf_op jit(solution)/shard_map/reshape | solution.py:63
  299.5 1.8 constant_dynamic-slice_fusion
  301.3 3.3 maximum_bitcast_fusion
  304.6 22.1 %fusion.78 = (bf16[2,4,512,2048]{2,3,0,1:T(8,128)(2,1)}, f32[2,4,512,2048]{2,3,0,1:T(8,128)}) fusion(bf16[1,4,512,512]{3,2,0,1:T(8,128)(2,1)S(1)} %get-tuple-element.234, bf16[1,4,512,512]{3,2,0,1:T(8,128)(2,1)} %get-tuple-element.235, bf16[4,2048,512,1]{2,1,0,3:T(8,128)(2,1)} %reshape.366), kind=kOutput, calls=%fused_computation.137 | convolution fusion | flops 8615100416 | bytes 62914560 | tf_op jit(solution)/shard_map/rcpk,cqk->rcpq/dot_general | solution.py:68
  326.7 31.8 %copy.45 = f32[2,4,512,2048]{3,2,0,1:T(8,128)} copy(f32[2,4,512,2048]{2,3,0,1:T(8,128)} %get-tuple-element.233) | data formatting | bytes 67108864
  358.5 381.5 %while.16 = (s32[]{:T(128)}, f32[4,512]{1,0:T(4,128)S(1)}, f32[4,512]{1,0:T(4,128)S(1)}, f32[4,512]{1,0:T(4,128)S(1)}, f32[4,512]{1,0:T(4,128)S(1)}, /*index=5*/...) while((s32[]{:T(128)}, f32[4,512]{1,0:T(4,128)S(1)}, ...), condition=%wide.region_3.4_spmd.clone, body=%wide.region_0.3_spmd.clone.sunk | while | flops 402845696 | bytes 68075792 | solution.py:94
  358.6 8.9 %all_gather.24 = f32[2,4,2048]{2,0,1:T(2,128)S(1)} all-gather(f32[2,4,512]{2,0,1:T(2,128)S(1)} %pad_maximum_fusion.5), channel_id=1, replica_groups=mesh['chan'=32,'blk'=4] {'blk'}, dimensions={2}, use_global_device_ids=true | all-gather | bytes 81920 | tf_op jit(solution)/shard_map/while/body/eval_jaxpr/all_gather | solution.py:80
  367.5 30.8 %convolution_bitcast_fusion.2 = f32[2,2,4,512]{3,1,0,2:T(2,128)S(1)} fusion(f32[2,4,512,2048]{3,2,0,1:T(8,128)} %get-tuple-element.328, f32[2,4,2048]{2,0,1:T(2,128)S(1)} %all_gather.24), kind=kOutput, calls=%fused_computation.clone.1 | convolution fusion | flops 201326592 | bytes 33652736 | tf_op jit(solution)/shard_map/while/body/eval_jaxpr/rcpq,scq->rscp/dot_general | solution.py:82
  398.6 6.8 all_gather.25
  405.4 30.8 %fusion.97 = f32[4,2,2,512]{3,1,2,0:T(2,128)S(1)} fusion(f32[2,4,512,2048]{3,2,0,1:T(8,128)} %get-tuple-element.328, f32[2,4,2048,1]{2,1,0,3:T(4,128)S(1)} %bitcast.201), kind=kOutput, calls=%fused_computation.2.clone.1 | convolution fusion | flops 201326592 | bytes 33652736 | tf_op jit(solution)/shard_map/while/body/eval_jaxpr/rcpq,scq->rscp/dot_general | solution.py:82
  436.6 6.8 all_gather.24
  443.3 30.8 %convolution_bitcast_fusion.2 = f32[2,2,4,512]{3,1,0,2:T(2,128)S(1)} fusion(f32[2,4,512,2048]{3,2,0,1:T(8,128)} %get-tuple-element.328, f32[2,4,2048]{2,0,1:T(2,128)S(1)} %all_gather.24), kind=kOutput, calls=%fused_computation.clone.1 | convolution fusion | flops 201326592 | bytes 33652736 | tf_op jit(solution)/shard_map/while/body/eval_jaxpr/rcpq,scq->rscp/dot_general | solution.py:82
  474.5 6.8 all_gather.25
  481.2 30.8 %fusion.97 = f32[4,2,2,512]{3,1,2,0:T(2,128)S(1)} fusion(f32[2,4,512,2048]{3,2,0,1:T(8,128)} %get-tuple-element.328, f32[2,4,2048,1]{2,1,0,3:T(4,128)S(1)} %bitcast.201), kind=kOutput, calls=%fused_computation.2.clone.1 | convolution fusion | flops 201326592 | bytes 33652736 | tf_op jit(solution)/shard_map/while/body/eval_jaxpr/rcpq,scq->rscp/dot_general | solution.py:82
  512.1 0.1 multiply_reduce_fusion.5
  512.4 6.8 all_gather.24
  519.2 30.8 %convolution_bitcast_fusion.2 = f32[2,2,4,512]{3,1,0,2:T(2,128)S(1)} fusion(f32[2,4,512,2048]{3,2,0,1:T(8,128)} %get-tuple-element.328, f32[2,4,2048]{2,0,1:T(2,128)S(1)} %all_gather.24), kind=kOutput, calls=%fused_computation.clone.1 | convolution fusion | flops 201326592 | bytes 33652736 | tf_op jit(solution)/shard_map/while/body/eval_jaxpr/rcpq,scq->rscp/dot_general | solution.py:82
  550.3 6.8 all_gather.25
  557.0 30.8 %fusion.97 = f32[4,2,2,512]{3,1,2,0:T(2,128)S(1)} fusion(f32[2,4,512,2048]{3,2,0,1:T(8,128)} %get-tuple-element.328, f32[2,4,2048,1]{2,1,0,3:T(4,128)S(1)} %bitcast.201), kind=kOutput, calls=%fused_computation.2.clone.1 | convolution fusion | flops 201326592 | bytes 33652736 | tf_op jit(solution)/shard_map/while/body/eval_jaxpr/rcpq,scq->rscp/dot_general | solution.py:82
  588.2 6.8 all_gather.24
  595.0 30.8 %convolution_bitcast_fusion.2 = f32[2,2,4,512]{3,1,0,2:T(2,128)S(1)} fusion(f32[2,4,512,2048]{3,2,0,1:T(8,128)} %get-tuple-element.328, f32[2,4,2048]{2,0,1:T(2,128)S(1)} %all_gather.24), kind=kOutput, calls=%fused_computation.clone.1 | convolution fusion | flops 201326592 | bytes 33652736 | tf_op jit(solution)/shard_map/while/body/eval_jaxpr/rcpq,scq->rscp/dot_general | solution.py:82
  626.1 6.8 all_gather.25
  632.9 30.8 %fusion.97 = f32[4,2,2,512]{3,1,2,0:T(2,128)S(1)} fusion(f32[2,4,512,2048]{3,2,0,1:T(8,128)} %get-tuple-element.328, f32[2,4,2048,1]{2,1,0,3:T(4,128)S(1)} %bitcast.201), kind=kOutput, calls=%fused_computation.2.clone.1 | convolution fusion | flops 201326592 | bytes 33652736 | tf_op jit(solution)/shard_map/while/body/eval_jaxpr/rcpq,scq->rscp/dot_general | solution.py:82
  664.1 6.8 all_gather.24
  670.8 30.8 %convolution_bitcast_fusion.2 = f32[2,2,4,512]{3,1,0,2:T(2,128)S(1)} fusion(f32[2,4,512,2048]{3,2,0,1:T(8,128)} %get-tuple-element.328, f32[2,4,2048]{2,0,1:T(2,128)S(1)} %all_gather.24), kind=kOutput, calls=%fused_computation.clone.1 | convolution fusion | flops 201326592 | bytes 33652736 | tf_op jit(solution)/shard_map/while/body/eval_jaxpr/rcpq,scq->rscp/dot_general | solution.py:82
  701.9 6.8 all_gather.25
  708.7 30.8 %fusion.97 = f32[4,2,2,512]{3,1,2,0:T(2,128)S(1)} fusion(f32[2,4,512,2048]{3,2,0,1:T(8,128)} %get-tuple-element.328, f32[2,4,2048,1]{2,1,0,3:T(4,128)S(1)} %bitcast.201), kind=kOutput, calls=%fused_computation.2.clone.1 | convolution fusion | flops 201326592 | bytes 33652736 | tf_op jit(solution)/shard_map/while/body/eval_jaxpr/rcpq,scq->rscp/dot_general | solution.py:82
  740.0 6.8 all_gather.19
  746.8 1.1 copy.46
  747.9 3.8 reshape.368
  751.7 18.3 %all-to-all-start.1 = ((f32[32,1,512]{2,1,0:T(1,128)}), f32[32,1,512]{2,1,0:T(1,128)S(1)}, u32[]{:S(2)}, u32[]{:S(2)}) async-start(f32[32,1,512]{2,1,0:T(1,128)} %reshape.368), calls=%async_computation.1 | async-start | bytes 131072 | tf_op jit(solution)/shard_map/all_to_all | solution.py:96
  770.0 21.5 %copy.48 = bf16[2,4,512,2048]{3,2,1,0:T(8,128)(2,1)} copy(bf16[2,4,512,2048]{2,3,0,1:T(8,128)(2,1)} %get-tuple-element.232) | data formatting | bytes 33554432
  791.5 0.5 broadcast.226
  792.0 0.8 reduce
  792.8 3.2 reshape.369
  796.1 1.9 copy.47
  798.0 0.7 copy.49
  (82 shorter events, 3.4 us)
Async XLA Ops:
  7.2 111.0 %all-gather.2.cloned.1.call-start = ((), (), s32[]{:S(2)}) async-start(), calls=%async_computation.2 | async-start | bytes 10485760 | tf_op jit(solution)/shard_map/all_gather | solution.py:58
  14.5 10.2 %copy-start = (s32[16]{0:T(128)S(1)}, s32[16]{0:T(128)}, u32[]{:S(2)}) copy-start(s32[16]{0:T(128)} %param.7) | copy-start | bytes 196
  129.7 125.3 %all-to-all-start = ((bf16[128,64,2,256]{3,1,2,0:T(8,128)(2,1)}), bf16[128,64,2,256]{3,1,2,0:T(8,128)(2,1)}, u32[]{:S(2)}, u32[]{:S(2)}) async-start(bf16[128,64,2,256]{3,1,2,0:T(8,128)(2,1)} %copy.43), calls=%async_computation | async-start | bytes 16777216 | tf_op jit(solution)/shard_map/all_to_all | solution.py:59
  751.7 39.8 %all-to-all-start.1 = ((f32[32,1,512]{2,1,0:T(1,128)}), f32[32,1,512]{2,1,0:T(1,128)S(1)}, u32[]{:S(2)}, u32[]{:S(2)}) async-start(f32[32,1,512]{2,1,0:T(1,128)} %reshape.368), calls=%async_computation.1 | async-start | bytes 131072 | tf_op jit(solution)/shard_map/all_to_all | solution.py:96
Sparse Core Ops, SparseCore 0:
  52.1 65.9 all-gather.1
where the time goes:
time: 808 us; the launch traced here: 806 us
  matrix products  357 us (44%)
  waiting for transfers between devices  183 us (23%)
  local copies, waits for them, and re-layouts  131 us (16%)
  blocking collectives  76.4 us (9%)
  starting transfers between devices  25.6 us (3%)
  other arithmetic  17 us (2%)
  between operations  14.2 us (2%)
    dot_general x10, matrix products, sweep(): products = jnp.einsum('rcpq,scq->rscp', correlation, probes, precision=high)  308 us
    all_to_all x1, waiting for transfers between devices, shards(): lax.all_to_all(grouped, 'chan', split_axis=0, concat_axis=1, tiled=True)  117 us
    all_gather x10, blocking collectives, sweep(): lax.all_gather(jnp.stack([probe_re, probe_im]), 'blk', axis=2, tiled=True)  69.7 us
    all_gather x1, waiting for transfers between devices, shards(): grouped = lax.all_gather(spectra, 'blk', axis=1, tiled=True)  66.1 us
    unnamed x7, local copies, waits for them, and re-layouts  61 us
    reshape x2, local copies, waits for them, and re-layouts, shards(): whole = turned.reshape(local_chans, all_inputs, 2 * SPECTRA)  28.1 us
    dot_general x1, matrix products, channelize(): jnp.einsum('itj,jrc->cirt', frames, table, preferred_element_type=jnp.flo...  27.3 us
    dot_general x1, matrix products, shards(): jnp.einsum('rcpk,cqk->rcpq', stacked, whole, preferred_element_type=jnp.f...  22.1 us
  transfers between devices with their start and end apart: 3, of which 2 were waited for; matrix products, arithmetic and copies ran while one was open for 3% of the time, Pallas kernels for 0%

commit v1 on v0

--- a/solution.py
+++ b/solution.py
@@ -56,7 +56,10 @@
     blk_count = lax.axis_size("blk")
     block_index = lax.axis_index("blk")
     grouped = lax.all_gather(spectra, "blk", axis=1, tiled=True)
-    turned = lax.all_to_all(grouped, "chan", split_axis=0, concat_axis=1, tiled=True)
+    turned = jnp.concatenate(
+        lax.all_to_all(jnp.stack(jnp.split(grouped, lax.axis_size("chan"), axis=0)), "chan", 0, 0),
+        axis=1,
+    )
     local_chans = turned.shape[0]
     all_inputs = turned.shape[1]
     row_count = all_inputs // blk_count

time: 808 us -> 857 us (1.061)
  local copies, waits for them, and re-layouts: 131 us -> 178 us
    unnamed x7 -> x38, local copies, waits for them, and re-layouts: 61 us -> 118 us
    another operation x0 -> x3, local copies, waits for them, and re-layouts: none -> 30 us  [the longest x2 28.1 us: shards(): whole = turned.reshape(local_chans, all_inputs, 2 * SPECTRA)]
    all_to_all x1 -> x0, local copies, waits for them, and re-layouts: 16.4 us -> none  [shards(): lax.all_to_all(grouped, 'chan', split_axis=0, concat_axis=1, tiled=True)]
    reshape x2 -> x1, local copies, waits for them, and re-layouts: 28.1 us -> 16.3 us  [shards(): jnp.concatenate(lax.all_to_all(jnp.stack(jnp.split(grouped, lax.axis_size...]
    all_gather x1 -> x0, local copies, waits for them, and re-layouts: 11.5 us -> none  [shards(): grouped = lax.all_gather(spectra, 'blk', axis=1, tiled=True)]
where the time goes in v1:
time: 857 us; the launch traced here: 853 us
  matrix products  357 us (42%)
  waiting for transfers between devices  183 us (21%)
  local copies, waits for them, and re-layouts  178 us (21%)
  blocking collectives  76.4 us (9%)
  starting transfers between devices  25.6 us (3%)
  other arithmetic  17 us (2%)
  between operations  14.2 us (2%)
    dot_general x10, matrix products, sweep(): products = jnp.einsum('rcpq,scq->rscp', correlation, probes, precision=high)  308 us
    unnamed x38, local copies, waits for them, and re-layouts  118 us
    all_to_all x1, waiting for transfers between devices, shards(): lax.all_to_all(jnp.stack(jnp.split(grouped, lax.axis_size('chan'), axis=0...  117 us
    all_gather x10, blocking collectives, sweep(): lax.all_gather(jnp.stack([probe_re, probe_im]), 'blk', axis=2, tiled=True)  69.7 us
    all_gather x1, waiting for transfers between devices, shards(): grouped = lax.all_gather(spectra, 'blk', axis=1, tiled=True)  66.1 us
    another operation x2, local copies, waits for them, and re-layouts, shards(): whole = turned.reshape(local_chans, all_inputs, 2 * SPECTRA)  28.1 us
    dot_general x1, matrix products, channelize(): jnp.einsum('itj,jrc->cirt', frames, table, preferred_element_type=jnp.flo...  27.3 us
    dot_general x1, matrix products, shards(): jnp.einsum('rcpk,cqk->rcpq', stacked, whole, preferred_element_type=jnp.f...  22.1 us
  transfers between devices with their start and end apart: 3, of which 2 were waited for; matrix products, arithmetic and copies ran while one was open for 3% of the time, Pallas kernels for 0%

profile of v1, /device:TPU:1, one launch (start us, length us, event | category | flops | bytes accessed | tf_op | source)
XLA Modules:
  0.0 853.0 jit_solution(15456298881398994020)
XLA Ops:
  8.6 5.9 convert_element_type.41
  14.5 10.1 %reshape.357 = f32[16,263,512]{2,1,0:T(8,128)} reshape(f32[16,134656]{1,0:T(8,128)} %convert_element_type.41) | data formatting | bytes 17235968 | tf_op jit(solution)/shard_map/reshape | solution.py:35
  24.6 27.3 %fusion.34 = bf16[128,16,2,256]{3,0,1,2:T(8,128)(2,1)} fusion(f32[16]{0:T(128)S(1)} %convert_multiply_fusion, f32[16,263,512]{2,1,0:T(8,128)} %reshape.357, f32[512]{0:T(512)S(1)} %get-tuple-element.223, f32[512]{0:T(512)S(1)} %get-tuple-element.224, f32[512]{0:T(512)S(1)} %get-tuple-element.225, f32[512]{0:T(512)S(1)} %get-tuple-element.226, ...), kind=kOutput, calls=%fused_computation.69 | convolution fusion | flops 1109917696 | bytes 69484608 | tf_op jit(solution)/shard_map/itj,jrc->cirt/dot_general | solution.py:40
  52.0 66.1 %all-gather.2.cloned.1.call-done = bf16[128,64,2,256]{3,0,1,2:T(8,128)(2,1)} async-done(((bf16[128,16,2,256]{3,0,1,2:T(8,128)(2,1)}), bf16[128,64,2,256]{3,0,1,2:T(8,128)(2,1)}) %all-gather.2.cloned.1.call-update) | async-done | bytes 8388624 | tf_op jit(solution)/shard_map/all_gather | solution.py:58
  119.9 1.9 fusion.70
  123.6 1.9 fusion.68
  127.3 1.9 fusion.66
  131.0 1.9 fusion.64
  134.7 1.9 fusion.62
  138.4 1.9 fusion.60
  142.1 1.9 fusion.58
  145.8 1.9 fusion.56
  149.5 1.9 fusion.54
  153.2 1.9 fusion.52
  177.2 7.3 all-to-all-start
  185.4 117.2 %all-to-all-done = bf16[32,4,64,2,256]{4,1,2,3,0:T(4,128)(2,1)} async-done(((bf16[32,4,64,2,256]{4,1,2,3,0:T(4,128)(2,1)}), bf16[32,4,64,2,256]{4,1,2,3,0:T(4,128)(2,1)}, u32[]{:S(2)}, u32[]{:S(2)}) %all-to-all-start) | async-done | bytes 8388640 | tf_op jit(solution)/shard_map/all_to_all | solution.py:60
  302.5 16.3 %copy.41 = bf16[4,32,64,2,256]{4,3,2,1,0:T(2,128)(2,1)} copy(bf16[4,32,64,2,256]{4,0,2,3,1:T(4,128)(2,1)} %bitcast.36) | data formatting | bytes 16777216 | tf_op jit(solution)/shard_map/reshape | solution.py:59
  318.8 14.1 %reshape_reshape.3 = bf16[4,2048,512]{2,1,0:T(8,128)(2,1)} reshape(bf16[4,32,64,2,256]{4,3,2,1,0:T(2,128)(2,1)} %copy.41) | data formatting | bytes 16777216 | tf_op jit(solution)/shard_map/reshape;reshape | solution.py:66
  332.9 14.1 %reshape.365 = bf16[4,2048,512,1]{2,1,0,3:T(8,128)(2,1)} reshape(bf16[4,32,64,2,256]{4,3,2,1,0:T(2,128)(2,1)} %copy.41) | data formatting | bytes 16777216 | tf_op jit(solution)/shard_map/reshape;reshape | solution.py:66
  348.8 3.3 maximum_bitcast_fusion
  352.1 22.1 %fusion.110 = (bf16[2,4,512,2048]{2,3,0,1:T(8,128)(2,1)}, f32[2,4,512,2048]{2,3,0,1:T(8,128)}) fusion(bf16[1,4,512,512]{3,2,0,1:T(8,128)(2,1)S(1)} %get-tuple-element.234, bf16[1,4,512,512]{3,2,0,1:T(8,128)(2,1)} %get-tuple-element.235, bf16[4,2048,512,1]{2,1,0,3:T(8,128)(2,1)} %reshape.365), kind=kOutput, calls=%fused_computation.200 | convolution fusion | flops 8615100416 | bytes 62914560 | tf_op jit(solution)/shard_map/rcpk,cqk->rcpq/dot_general | solution.py:71
  374.2 31.8 %copy.42 = f32[2,4,512,2048]{3,2,0,1:T(8,128)} copy(f32[2,4,512,2048]{2,3,0,1:T(8,128)} %get-tuple-element.233) | data formatting | bytes 67108864
  406.0 381.5 %while.16 = (s32[]{:T(128)}, f32[4,512]{1,0:T(4,128)S(1)}, f32[4,512]{1,0:T(4,128)S(1)}, f32[4,512]{1,0:T(4,128)S(1)}, f32[4,512]{1,0:T(4,128)S(1)}, /*index=5*/...) while((s32[]{:T(128)}, f32[4,512]{1,0:T(4,128)S(1)}, ...), condition=%wide.region_3.4_spmd.clone, body=%wide.region_0.3_spmd.clone.sunk | while | flops 402845696 | bytes 68075792 | solution.py:97
  406.0 8.9 %all_gather.24 = f32[2,4,2048]{2,0,1:T(2,128)S(1)} all-gather(f32[2,4,512]{2,0,1:T(2,128)S(1)} %pad_maximum_fusion.5), channel_id=1, replica_groups=mesh['chan'=32,'blk'=4] {'blk'}, dimensions={2}, use_global_device_ids=true | all-gather | bytes 81920 | tf_op jit(solution)/shard_map/while/body/eval_jaxpr/all_gather | solution.py:83
  415.0 30.8 %convolution_bitcast_fusion.2 = f32[2,2,4,512]{3,1,0,2:T(2,128)S(1)} fusion(f32[2,4,512,2048]{3,2,0,1:T(8,128)} %get-tuple-element.328, f32[2,4,2048]{2,0,1:T(2,128)S(1)} %all_gather.24), kind=kOutput, calls=%fused_computation.clone.1 | convolution fusion | flops 201326592 | bytes 33652736 | tf_op jit(solution)/shard_map/while/body/eval_jaxpr/rcpq,scq->rscp/dot_general | solution.py:85
  446.1 6.8 all_gather.25
  452.8 30.8 %fusion.129 = f32[4,2,2,512]{3,1,2,0:T(2,128)S(1)} fusion(f32[2,4,512,2048]{3,2,0,1:T(8,128)} %get-tuple-element.328, f32[2,4,2048,1]{2,1,0,3:T(4,128)S(1)} %bitcast.324), kind=kOutput, calls=%fused_computation.2.clone.1 | convolution fusion | flops 201326592 | bytes 33652736 | tf_op jit(solution)/shard_map/while/body/eval_jaxpr/rcpq,scq->rscp/dot_general | solution.py:85
  484.0 6.8 all_gather.24
  490.8 30.8 %convolution_bitcast_fusion.2 = f32[2,2,4,512]{3,1,0,2:T(2,128)S(1)} fusion(f32[2,4,512,2048]{3,2,0,1:T(8,128)} %get-tuple-element.328, f32[2,4,2048]{2,0,1:T(2,128)S(1)} %all_gather.24), kind=kOutput, calls=%fused_computation.clone.1 | convolution fusion | flops 201326592 | bytes 33652736 | tf_op jit(solution)/shard_map/while/body/eval_jaxpr/rcpq,scq->rscp/dot_general | solution.py:85
  521.9 6.8 all_gather.25
  528.7 30.8 %fusion.129 = f32[4,2,2,512]{3,1,2,0:T(2,128)S(1)} fusion(f32[2,4,512,2048]{3,2,0,1:T(8,128)} %get-tuple-element.328, f32[2,4,2048,1]{2,1,0,3:T(4,128)S(1)} %bitcast.324), kind=kOutput, calls=%fused_computation.2.clone.1 | convolution fusion | flops 201326592 | bytes 33652736 | tf_op jit(solution)/shard_map/while/body/eval_jaxpr/rcpq,scq->rscp/dot_general | solution.py:85
  559.9 6.8 all_gather.24
  566.6 30.8 %convolution_bitcast_fusion.2 = f32[2,2,4,512]{3,1,0,2:T(2,128)S(1)} fusion(f32[2,4,512,2048]{3,2,0,1:T(8,128)} %get-tuple-element.328, f32[2,4,2048]{2,0,1:T(2,128)S(1)} %all_gather.24), kind=kOutput, calls=%fused_computation.clone.1 | convolution fusion | flops 201326592 | bytes 33652736 | tf_op jit(solution)/shard_map/while/body/eval_jaxpr/rcpq,scq->rscp/dot_general | solution.py:85
  597.7 6.8 all_gather.25
  604.5 30.8 %fusion.129 = f32[4,2,2,512]{3,1,2,0:T(2,128)S(1)} fusion(f32[2,4,512,2048]{3,2,0,1:T(8,128)} %get-tuple-element.328, f32[2,4,2048,1]{2,1,0,3:T(4,128)S(1)} %bitcast.324), kind=kOutput, calls=%fused_computation.2.clone.1 | convolution fusion | flops 201326592 | bytes 33652736 | tf_op jit(solution)/shard_map/while/body/eval_jaxpr/rcpq,scq->rscp/dot_general | solution.py:85
  635.7 6.8 all_gather.24
  642.4 30.8 %convolution_bitcast_fusion.2 = f32[2,2,4,512]{3,1,0,2:T(2,128)S(1)} fusion(f32[2,4,512,2048]{3,2,0,1:T(8,128)} %get-tuple-element.328, f32[2,4,2048]{2,0,1:T(2,128)S(1)} %all_gather.24), kind=kOutput, calls=%fused_computation.clone.1 | convolution fusion | flops 201326592 | bytes 33652736 | tf_op jit(solution)/shard_map/while/body/eval_jaxpr/rcpq,scq->rscp/dot_general | solution.py:85
  673.6 6.8 all_gather.25
  680.3 30.8 %fusion.129 = f32[4,2,2,512]{3,1,2,0:T(2,128)S(1)} fusion(f32[2,4,512,2048]{3,2,0,1:T(8,128)} %get-tuple-element.328, f32[2,4,2048,1]{2,1,0,3:T(4,128)S(1)} %bitcast.324), kind=kOutput, calls=%fused_computation.2.clone.1 | convolution fusion | flops 201326592 | bytes 33652736 | tf_op jit(solution)/shard_map/while/body/eval_jaxpr/rcpq,scq->rscp/dot_general | solution.py:85
  711.5 6.8 all_gather.24
  718.3 30.8 %convolution_bitcast_fusion.2 = f32[2,2,4,512]{3,1,0,2:T(2,128)S(1)} fusion(f32[2,4,512,2048]{3,2,0,1:T(8,128)} %get-tuple-element.328, f32[2,4,2048]{2,0,1:T(2,128)S(1)} %all_gather.24), kind=kOutput, calls=%fused_computation.clone.1 | convolution fusion | flops 201326592 | bytes 33652736 | tf_op jit(solution)/shard_map/while/body/eval_jaxpr/rcpq,scq->rscp/dot_general | solution.py:85
  749.4 6.8 all_gather.25
  756.1 30.8 %fusion.129 = f32[4,2,2,512]{3,1,2,0:T(2,128)S(1)} fusion(f32[2,4,512,2048]{3,2,0,1:T(8,128)} %get-tuple-element.328, f32[2,4,2048,1]{2,1,0,3:T(4,128)S(1)} %bitcast.324), kind=kOutput, calls=%fused_computation.2.clone.1 | convolution fusion | flops 201326592 | bytes 33652736 | tf_op jit(solution)/shard_map/while/body/eval_jaxpr/rcpq,scq->rscp/dot_general | solution.py:85
  787.5 6.8 all_gather.19
  795.3 3.8 reshape.367
  799.1 18.3 %all-to-all-start.1 = ((f32[32,1,512]{2,1,0:T(1,128)}), f32[32,1,512]{2,1,0:T(1,128)S(1)}, u32[]{:S(2)}, u32[]{:S(2)}) async-start(f32[32,1,512]{2,1,0:T(1,128)} %reshape.367), calls=%async_computation.1 | async-start | bytes 131072 | tf_op jit(solution)/shard_map/all_to_all | solution.py:99
  817.4 21.5 %copy.45 = bf16[2,4,512,2048]{3,2,1,0:T(8,128)(2,1)} copy(bf16[2,4,512,2048]{2,3,0,1:T(8,128)(2,1)} %get-tuple-element.232) | data formatting | bytes 33554432
  840.3 3.2 reshape.368
  (113 shorter events, 52.6 us)
Async XLA Ops:
  7.2 111.0 %all-gather.2.cloned.1.call-start = ((), (), s32[]{:S(2)}) async-start(), calls=%async_computation.2 | async-start | bytes 10485760 | tf_op jit(solution)/shard_map/all_gather | solution.py:58
  14.5 10.2 %copy-start = (s32[16]{0:T(128)S(1)}, s32[16]{0:T(128)}, u32[]{:S(2)}) copy-start(s32[16]{0:T(128)} %param.7) | copy-start | bytes 196
  177.2 125.3 %all-to-all-start = ((bf16[32,4,64,2,256]{4,1,2,3,0:T(4,128)(2,1)}), bf16[32,4,64,2,256]{4,1,2,3,0:T(4,128)(2,1)}, u32[]{:S(2)}, u32[]{:S(2)}) async-start(bf16[32,4,64,2,256]{4,1,2,3,0:T(4,128)(2,1)} %fusion.40), calls=%async_computation | async-start | bytes 16777216 | tf_op jit(solution)/shard_map/all_to_all | solution.py:60
  799.1 39.8 %all-to-all-start.1 = ((f32[32,1,512]{2,1,0:T(1,128)}), f32[32,1,512]{2,1,0:T(1,128)S(1)}, u32[]{:S(2)}, u32[]{:S(2)}) async-start(f32[32,1,512]{2,1,0:T(1,128)} %reshape.367), calls=%async_computation.1 | async-start | bytes 131072 | tf_op jit(solution)/shard_map/all_to_all | solution.py:99
Sparse Core Ops, SparseCore 0:
  52.1 65.9 all-gather.1
